TPU v7x, 32 devices: a whole 2x2x4 slice. The times are simulated.
32 devices in a mesh: group: 4 (over y, core), tile: 8 (over z, x).
Axes of the slice: x: 2, y: 2, z: 4, core: 2. Of those that a mesh axis runs over, the one named last changes fastest.
Arguments:
- maps: bfloat16 [32, 256, 128, 128], P('group', 'tile'), may hold values from -6 to 6
- first_weight: bfloat16 [3, 3, 128, 256], replicated, may hold values from -0.1875 to 0.1875
- second_weight: bfloat16 [3, 3, 256, 256], replicated, may hold values from -0.125 to 0.125
- out_grad: bfloat16 [32, 128, 64, 256], P(('group', 'tile')), may hold values from -0.0234375 to 0.0234375
Outputs:
- conv_out: bfloat16 [32, 128, 64, 256], P(('group', 'tile'))
- weight_grad: float32 [256, 3, 3, 256], P(('group', 'tile'))
All inputs are finite; a program needn't handle non-finite values.
Results may differ from a plain program's by a relative error of at most 0.0051.
Values may be sent and summed in bfloat16 or wider, within the bound.
No kernel may reach another device: no remote copies, remote signals or barrier semaphores. Data moves between devices by JAX's collectives and lax.ppermute only.
A program may use at most 192 MiB of HBM per device.

v0:
```python
import jax
import jax.numpy as jnp
from jax import lax
from jax.sharding import PartitionSpec as P


def shifted_2(shard, axis, by):
    length = lax.axis_size(axis)
    pairs = [(i, i + by) for i in range(length) if 0 <= i + by < length]
    return lax.ppermute(shard, axis, pairs)


def shift_cols_right(slab):
    zero_col = jnp.zeros_like(slab[:, :, :1])
    return jnp.concatenate([zero_col, slab[:, :, :-1]], axis=2)


def shift_cols_left(slab):
    zero_col = jnp.zeros_like(slab[:, :, :1])
    return jnp.concatenate([slab[:, :, 1:], zero_col], axis=2)


def first_conv(source, upper_row, first_weight):
    images, rows, width, inputs = source.shape
    outputs = first_weight.shape[3]
    paired = source.reshape(images, rows // 2, 2, width // 2, 2 * inputs)
    even_rows = paired[:, :, 0]
    odd_rows = paired[:, :, 1]
    upper_paired = upper_row.reshape(images, 1, width // 2, 2 * inputs)
    odd_above = jnp.concatenate([upper_paired, odd_rows[:, :-1]], axis=1)
    sources = [odd_above, even_rows, odd_rows]
    total = jnp.zeros((images, rows // 2, width // 2, outputs), jnp.float32)
    for tap_row in range(3):
        wide_kernel = first_weight[tap_row, 1:3].reshape(2 * inputs, outputs)
        total = total + jnp.dot(sources[tap_row], wide_kernel, preferred_element_type=jnp.float32)
    halves = jnp.concatenate([piece[..., inputs:] for piece in sources], axis=-1)
    narrow_kernel = first_weight[:, 0].reshape(3 * inputs, outputs)
    total = total + jnp.dot(
        shift_cols_right(halves), narrow_kernel, preferred_element_type=jnp.float32
    )
    return jnp.maximum(total, 0.0).astype(jnp.bfloat16)


def local(maps, first_weight, second_weight, out_grad):
    tiles = lax.axis_size("tile")
    images, height, width, inputs = maps.shape
    outputs = first_weight.shape[3]
    owned = images // tiles
    upper_row = shifted_2(maps[:, height - 1 : height], "tile", 1)
    local_hidden = first_conv(maps, upper_row, first_weight)
    half_rows = height // 2
    arrived = lax.all_to_all(
        local_hidden.reshape(tiles, owned, half_rows, width // 2, outputs),
        "tile",
        split_axis=0,
        concat_axis=2,
        tiled=True,
    )
    hidden = arrived.reshape(owned, half_rows * tiles, width // 2, outputs)
    out_rows = hidden.shape[1]
    out_cols = hidden.shape[2]
    row_padded = jnp.pad(hidden, ((0, 0), (1, 1), (0, 0), (0, 0)))
    shifted = [shift_cols_right(row_padded), row_padded, shift_cols_left(row_padded)]
    total = jnp.zeros((owned, out_rows, out_cols, outputs), jnp.float32)
    for tap_row in range(3):
        for tap_col in range(3):
            window = shifted[tap_col][:, tap_row : tap_row + out_rows]
            total = total + jnp.dot(
                window, second_weight[tap_row, tap_col], preferred_element_type=jnp.float32
            )
    conv_out = total.astype(jnp.bfloat16)
    devices = lax.axis_size("group") * tiles
    selected = out_grad.reshape(-1, lax.axis_size(("group", "tile")) * (outputs // devices))
    terms = []
    for tap_row in range(3):
        for tap_col in range(3):
            window = shifted[tap_col][:, tap_row : tap_row + out_rows].reshape(-1, outputs)
            terms.append(
                lax.dot_general(
                    selected, window, (((0,), (0,)), ((), ())), preferred_element_type=jnp.float32
                )
            )
    summed = lax.psum_scatter(
        jnp.stack(terms, axis=1).reshape(
            lax.axis_size(("group", "tile")) * (outputs // devices), 9 * outputs
        ),
        ("group", "tile"),
        scatter_dimension=0,
        tiled=True,
    )
    weight_grad = summed.reshape(-1, 3, 3, outputs)
    return (conv_out, weight_grad)


def solution(mesh):
    return jax.shard_map(
        local,
        mesh=mesh,
        in_specs=(P("group", "tile", None, None), P(), P(), P(("group", "tile"), None, None, None)),
        out_specs=(P(("group", "tile"), None, None, None), P(("group", "tile"), None, None, None)),
        check_vma=False,
    )
```

profile of v0, /device:TPU:0, one launch (start us, length us, event | category | flops | bytes accessed | tf_op | source)
XLA Modules:
  0.0 348.4 jit_solution(9022107546819320369)
XLA Ops:
  7.2 0.0 reduce-scatter.2.cloned.1.call-start
  7.2 1.0 slice.103
  8.2 0.0 copy-start.4
  8.2 5.0 %collective-permute-start = (bf16[8,1,128,128]{3,2,1,0:T(8,128)(2,1)S(1)}, bf16[8,1,128,128]{3,2,1,0:T(8,128)(2,1)S(1)}, u32[]{:S(2)}, u32[]{:S(2)}) collective-permute-start(bf16[8,1,128,128]{3,2,1,0:T(8,128)(2,1)S(1)} %slice.103), channel_id=1, source_target_pairs={{0,1},{1,2},{2,3},{3,4},{4,5},{5,6},{6,7},{8,9},{9,10},{10,11},{11... | collective-permute-start | bytes 786440 | tf_op jit(solution)/shard_map/ppermute | solution.py:10
  13.2 12.9 %reshape.106 = bf16[8,16,2,64,256]{4,3,2,1,0:T(8,128)(2,1)} reshape(bf16[8,32,128,128]{3,2,1,0:T(8,128)(2,1)} %param.4) | data formatting | bytes 16777216 | tf_op jit(solution)/shard_map/reshape | solution.py:26
  26.1 0.0 copy-done.4
  26.2 0.0 slice-start
  26.2 0.0 slice-start.1
  26.2 6.8 %fusion.185 = f32[8,16,64,256]{3,2,1,0:T(8,128)} fusion(bf16[256,256,1,1]{1,0,3,2:T(8,128)(2,1)S(1)} %bitcast.263, bf16[8,16,2,64,256]{4,3,2,1,0:T(8,128)(2,1)} %reshape.106), kind=kOutput, calls=%fused_computation.155 | convolution fusion | flops 1073741824 | bytes 12713984 | tf_op jit(solution)/shard_map/dot_general | solution.py:35
  33.0 0.0 slice-done
  33.0 0.0 slice-done.1
  33.0 4.5 %fusion.186 = f32[8,16,64,256]{3,2,1,0:T(8,128)} fusion(bf16[256,256,1,1]{1,0,3,2:T(8,128)(2,1)S(1)} %bitcast.262, bf16[8,16,2,64,256]{4,3,2,1,0:T(8,128)(2,1)S(1)} %bitcast.242), kind=kOutput, calls=%fused_computation.156 | convolution fusion | flops 1073741824 | bytes 12713984 | tf_op jit(solution)/shard_map/dot_general | solution.py:35
  37.5 1.2 slice_bitcast_fusion
  38.7 2.4 slice.135
  41.1 1.8 slice.138
  42.9 1.8 slice.137
  44.7 0.0 collective-permute-done
  44.7 0.1 reshape.105
  44.8 0.0 copy-start.1
  44.8 0.0 slice-start.2
  44.8 3.5 %fusion.19 = f32[8,16,64,256]{3,2,1,0:T(8,128)S(1)} fusion(bf16[256,256,1,1]{1,0,3,2:T(8,128)(2,1)S(1)} %bitcast.261, bf16[8,15,64,256]{3,2,1,0:T(8,128)(2,1)} %slice.135, bf16[8,1,64,256]{3,2,1,0:T(8,128)(2,1)S(1)} %reshape.105), kind=kOutput, calls=%fused_computation.20 | convolution fusion | flops 1075838976 | bytes 12713984 | tf_op jit(solution)/shard_map/dot_general | solution.py:35
  48.3 0.0 copy-done.1
  48.3 0.0 slice-done.2
  48.3 10.3 %fusion.17 = bf16[8,1,16,64,256]{4,3,2,1,0:T(8,128)(2,1)} fusion(f32[8,16,64,256]{3,2,1,0:T(8,128)} %fusion.185, f32[8,16,64,256]{3,2,1,0:T(8,128)S(1)} %fusion.19, f32[8,16,64,256]{3,2,1,0:T(8,128)} %fusion.186, bf16[384,256,1,1]{1,0,3,2:T(8,128)(2,1)S(1)} %bitcast.260, bf16[8,16,64,128]{3,2,1,0:T(8,128)(2,1)} %slice.138, ...), kind=kOutput, calls=%fused_computation.16 | convolution fusion | flops 1661992960 | bytes 37945344 | tf_op jit(solution)/shard_map/dot_general | solution.py:38
  58.6 98.4 %all_to_all.4 = bf16[8,1,16,64,256]{4,3,2,1,0:T(8,128)(2,1)S(1)} all-to-all(bf16[8,1,16,64,256]{4,3,2,1,0:T(8,128)(2,1)} %fusion.17), channel_id=1, replica_groups=mesh['group'=4,'tile'=8] {'tile'}, dimensions={0} | all-to-all | bytes 8388608 | tf_op jit(solution)/shard_map/all_to_all | solution.py:52
  157.1 2.4 copy.51
  159.5 0.0 copy-start
  159.5 0.0 copy-start.3
  159.5 4.8 %pad_slice_fusion.1 = (bf16[1,130,63,256]{3,1,2,0:T(8,128)(2,1)S(1)}, bf16[1,130,63,256]{3,1,2,0:T(8,128)(2,1)S(1)}) fusion(bf16[1,128,64,256]{3,1,2,0:T(8,128)(2,1)S(1)} %bitcast.243), kind=kLoop, calls=%fused_computation.78 | loop fusion | bytes 12580864 | tf_op jit(solution)/shard_map/slice | solution.py:15
  164.4 0.0 copy-done.3
  164.4 4.5 %fusion.25 = f32[128,64,256]{2,0,1:T(8,128)} fusion(bf16[1,130,63,256]{3,1,2,0:T(8,128)(2,1)S(1)} %get-tuple-element.11, bf16[3,3,256,256]{3,2,1,0:T(8,128)(2,1)S(1)} %copy-done.3), kind=kOutput, calls=%fused_computation.26 | convolution fusion | flops 1073741824 | bytes 12906496 | tf_op jit(solution)/shard_map/dot_general | solution.py:68
  168.9 4.5 %fusion.37 = f32[128,64,256]{2,0,1:T(8,128)} fusion(bf16[1,130,63,256]{3,1,2,0:T(8,128)(2,1)S(1)} %get-tuple-element.11, bf16[3,3,256,256]{3,2,1,0:T(8,128)(2,1)S(1)} %copy-done.3), kind=kOutput, calls=%fused_computation.38 | convolution fusion | flops 1073741824 | bytes 12906496 | tf_op jit(solution)/shard_map/dot_general | solution.py:68
  173.4 4.5 %fusion.33 = f32[128,64,256]{2,0,1:T(8,128)} fusion(bf16[1,130,63,256]{3,1,2,0:T(8,128)(2,1)S(1)} %get-tuple-element.10, bf16[3,3,256,256]{3,2,1,0:T(8,128)(2,1)S(1)} %copy-done.3), kind=kOutput, calls=%fused_computation.34 | convolution fusion | flops 1073741824 | bytes 12906496 | tf_op jit(solution)/shard_map/dot_general | solution.py:68
  177.8 4.5 %fusion.41 = f32[128,64,256]{2,0,1:T(8,128)} fusion(bf16[1,130,63,256]{3,1,2,0:T(8,128)(2,1)S(1)} %get-tuple-element.10, bf16[3,3,256,256]{3,2,1,0:T(8,128)(2,1)S(1)} %copy-done.3), kind=kOutput, calls=%fused_computation.42 | convolution fusion | flops 1073741824 | bytes 12906496 | tf_op jit(solution)/shard_map/dot_general | solution.py:68
  182.3 4.5 %fusion.45 = f32[128,64,256]{2,0,1:T(8,128)} fusion(bf16[1,130,63,256]{3,1,2,0:T(8,128)(2,1)S(1)} %get-tuple-element.11, bf16[3,3,256,256]{3,2,1,0:T(8,128)(2,1)S(1)} %copy-done.3), kind=kOutput, calls=%fused_computation.46 | convolution fusion | flops 1073741824 | bytes 12906496 | tf_op jit(solution)/shard_map/dot_general | solution.py:68
  186.8 4.5 %fusion.53 = f32[128,64,256]{2,0,1:T(8,128)} fusion(bf16[1,130,63,256]{3,1,2,0:T(8,128)(2,1)S(1)} %get-tuple-element.10, bf16[3,3,256,256]{3,2,1,0:T(8,128)(2,1)S(1)} %copy-done.3), kind=kOutput, calls=%fused_computation.54 | convolution fusion | flops 1073741824 | bytes 12906496 | tf_op jit(solution)/shard_map/dot_general | solution.py:68
  191.3 0.0 copy-start.2
  191.3 4.5 %fusion.29 = f32[128,64,256]{2,0,1:T(8,128)} fusion(bf16[1,128,64,256]{3,1,2,0:T(8,128)(2,1)S(1)} %bitcast.244, bf16[3,3,256,256]{3,2,1,0:T(8,128)(2,1)S(1)} %copy-done.3), kind=kOutput, calls=%fused_computation.30 | convolution fusion | flops 1073741824 | bytes 12713984 | tf_op jit(solution)/shard_map/dot_general | solution.py:68
  195.8 0.0 copy-done.2
  195.8 5.1 %fusion.93 = f32[256,9,256]{0,2,1:T(8,128)S(1)} fusion(bf16[1,130,63,256]{3,1,2,0:T(8,128)(2,1)S(1)} %get-tuple-element.10, bf16[128,64,256]{2,1,0:T(8,128)(2,1)S(1)} %bitcast.250), kind=kOutput, calls=%fused_computation.92 | convolution fusion | flops 1073741824 | bytes 8649728 | tf_op jit(solution)/shard_map/dot_general | solution.py:79
  200.9 5.6 %fusion.99 = f32[256,9,256]{0,2,1:T(8,128)S(1)} fusion(f32[256,9,256]{0,2,1:T(8,128)S(1)} %fusion.93, bf16[1,128,64,256]{3,1,2,0:T(8,128)(2,1)S(1)} %bitcast.245, bf16[128,64,256]{2,1,0:T(8,128)(2,1)S(1)} %bitcast.251), kind=kOutput, calls=%fused_computation.94 | convolution fusion | flops 1073741824 | bytes 8650752 | tf_op jit(solution)/shard_map/dot_general | solution.py:79
  206.5 5.3 %fusion.105 = f32[256,9,256]{0,2,1:T(8,128)S(1)} fusion(f32[256,9,256]{0,2,1:T(8,128)S(1)} %fusion.99, bf16[1,130,63,256]{3,1,2,0:T(8,128)(2,1)S(1)} %get-tuple-element.11, bf16[128,64,256]{2,1,0:T(8,128)(2,1)S(1)} %bitcast.252), kind=kOutput, calls=%fused_computation.96 | convolution fusion | flops 1073741824 | bytes 8843264 | tf_op jit(solution)/shard_map/dot_general | solution.py:79
  211.8 5.5 %fusion.111 = f32[256,9,256]{0,2,1:T(8,128)S(1)} fusion(f32[256,9,256]{0,2,1:T(8,128)S(1)} %fusion.105, bf16[1,130,63,256]{3,1,2,0:T(8,128)(2,1)S(1)} %get-tuple-element.10, bf16[128,64,256]{2,1,0:T(8,128)(2,1)S(1)} %bitcast.253), kind=kOutput, calls=%fused_computation.98 | convolution fusion | flops 1073741824 | bytes 8843264 | tf_op jit(solution)/shard_map/dot_general | solution.py:79
  217.3 1.3 fusion.138
  218.7 5.6 %fusion.117 = f32[256,9,256]{0,2,1:T(8,128)S(1)} fusion(f32[256,9,256]{0,2,1:T(8,128)S(1)} %fusion.138, bf16[1,130,63,256]{3,1,2,0:T(8,128)(2,1)S(1)} %get-tuple-element.11, bf16[128,64,256]{2,1,0:T(8,128)(2,1)S(1)} %bitcast.255), kind=kOutput, calls=%fused_computation.100 | convolution fusion | flops 1073741824 | bytes 8843264 | tf_op jit(solution)/shard_map/dot_general | solution.py:79
  224.3 5.7 %fusion.123 = f32[256,9,256]{0,2,1:T(8,128)S(1)} fusion(f32[256,9,256]{0,2,1:T(8,128)S(1)} %fusion.117, bf16[1,130,63,256]{3,1,2,0:T(8,128)(2,1)S(1)} %get-tuple-element.10, bf16[128,64,256]{2,1,0:T(8,128)(2,1)S(1)} %bitcast.256), kind=kOutput, calls=%fused_computation.102 | convolution fusion | flops 1073741824 | bytes 8843264 | tf_op jit(solution)/shard_map/dot_general | solution.py:79
  230.0 0.0 copy-done
  230.0 5.6 %fusion.129 = f32[256,9,256]{0,2,1:T(8,128)S(1)} fusion(f32[256,9,256]{0,2,1:T(8,128)S(1)} %fusion.123, bf16[1,128,64,256]{3,1,2,0:T(8,128)(2,1)S(1)} %bitcast.246, bf16[128,64,256]{2,1,0:T(8,128)(2,1)S(1)} %bitcast.257), kind=kOutput, calls=%fused_computation.104 | convolution fusion | flops 1073741824 | bytes 8650752 | tf_op jit(solution)/shard_map/dot_general | solution.py:79
  235.6 5.7 %fusion.135 = f32[256,9,256]{0,2,1:T(8,128)S(1)} fusion(f32[256,9,256]{0,2,1:T(8,128)S(1)} %fusion.129, bf16[1,130,63,256]{3,1,2,0:T(8,128)(2,1)S(1)} %get-tuple-element.11, bf16[128,64,256]{2,1,0:T(8,128)(2,1)S(1)} %bitcast.258), kind=kOutput, calls=%fused_computation.106 | convolution fusion | flops 1073741824 | bytes 8843264 | tf_op jit(solution)/shard_map/dot_general | solution.py:79
  241.4 2.0 copy.69
  243.3 0.0 reduce-scatter.2.cloned.1.call-update
  243.4 6.7 %fusion.49 = f32[128,64,256]{2,0,1:T(8,128)} fusion(bf16[1,128,64,256]{3,1,2,0:T(8,128)(2,1)} %bitcast.247, bf16[3,3,256,256]{3,2,1,0:T(8,128)(2,1)S(1)} %copy-done.3), kind=kOutput, calls=%fused_computation.50 | convolution fusion | flops 1073741824 | bytes 12713984 | tf_op jit(solution)/shard_map/dot_general | solution.py:68
  250.1 25.8 %fusion.18 = bf16[1,128,64,256]{3,1,2,0:T(8,128)(2,1)} fusion(f32[128,64,256]{2,0,1:T(8,128)} %fusion.25, f32[128,64,256]{2,0,1:T(8,128)} %fusion.29, f32[128,64,256]{2,0,1:T(8,128)} %fusion.33, f32[128,64,256]{2,0,1:T(8,128)} %fusion.37, f32[128,64,256]{2,0,1:T(8,128)} %fusion.41, f32[128,64,256]{2,0,1:T(8,128)} %fusion.45, f32[128,64,256]{2,0,1:T(8,128)} %fusion.53, ...), kind=kOutput, calls=%fused_computation.17 | convolution fusion | flops 1092616192 | bytes 75628544 | tf_op jit(solution)/shard_map/dot_general | solution.py:68
  275.9 6.6 %copy.70 = bf16[1,128,64,256]{3,2,1,0:T(8,128)(2,1)} copy(bf16[1,128,64,256]{3,1,2,0:T(8,128)(2,1)} %fusion.18) | data formatting | bytes 8388608
  282.5 58.8 %reduce-scatter.2.cloned.1.call-done = f32[8,2304]{1,0:T(8,128)} async-done(((f32[256,2304]{1,0:T(8,128)}), f32[8,2304]{1,0:T(8,128)}) %reduce-scatter.2.cloned.1.call-update) | async-done | bytes 73744 | tf_op jit(solution)/shard_map/reduce_scatter | solution.py:83
  (2 shorter events, 0.0 us)
Async XLA Ops:
  7.2 334.2 %reduce-scatter.2.cloned.1.call-start = ((), (), s32[]{:S(2)}) async-start(), calls=%async_computation.2 | async-start | bytes 2433024 | tf_op jit(solution)/shard_map/reduce_scatter | solution.py:83
  8.2 17.9 %copy-start.4 = (bf16[3,3,128,256]{3,2,1,0:T(8,128)(2,1)S(1)}, bf16[3,3,128,256]{3,2,1,0:T(8,128)(2,1)}, u32[]{:S(2)}) copy-start(bf16[3,3,128,256]{3,2,1,0:T(8,128)(2,1)} %param.5) | copy-start | bytes 1769476
  8.2 36.5 %collective-permute-start = (bf16[8,1,128,128]{3,2,1,0:T(8,128)(2,1)S(1)}, bf16[8,1,128,128]{3,2,1,0:T(8,128)(2,1)S(1)}, u32[]{:S(2)}, u32[]{:S(2)}) collective-permute-start(bf16[8,1,128,128]{3,2,1,0:T(8,128)(2,1)S(1)} %slice.103), channel_id=1, source_target_pairs={{0,1},{1,2},{2,3},{3,4},{4,5},{5,6},{6,7},{8,9},{9,10},{10,11},{11... | collective-permute-start | bytes 786440 | tf_op jit(solution)/shard_map/ppermute | solution.py:10
  26.2 6.9 %slice-start = ((s8[8388608]{0:T(1024)(128)(4,1)}), s8[4194304]{0:T(1024)(128)(4,1)S(1)}, s32[]{:S(2)}) async-start(s8[8388608]{0:T(1024)(128)(4,1)} %bitcast.241), calls=%async_computation.3 | async-start | bytes 8388608
  26.2 6.8 %slice-start.1 = ((s8[8388608]{0:T(1024)(128)(4,1)}), s8[4194304]{0:T(1024)(128)(4,1)S(1)}, s32[]{:S(2)}) async-start(s8[8388608]{0:T(1024)(128)(4,1)} %bitcast.241), calls=%async_computation.4 | async-start | bytes 8388608
  44.8 3.5 %copy-start.1 = (bf16[8,15,64,256]{3,2,1,0:T(8,128)(2,1)S(1)}, bf16[8,15,64,256]{3,2,1,0:T(8,128)(2,1)}, u32[]{:S(2)}) copy-start(bf16[8,15,64,256]{3,2,1,0:T(8,128)(2,1)} %slice.135) | copy-start | bytes 11796484
  44.8 3.5 %slice-start.2 = ((bf16[3,3,128,256]{3,2,1,0:T(8,128)(2,1)}), bf16[3,1,128,256]{3,2,1,0:T(8,128)(2,1)S(1)}, s32[]{:S(2)}) async-start(bf16[3,3,128,256]{3,2,1,0:T(8,128)(2,1)} %param.5), calls=%async_computation.5 | async-start | bytes 393216 | tf_op jit(solution)/shard_map/slice | solution.py:37
  159.5 70.5 %copy-start = (bf16[8,1,16,64,256]{4,2,0,3,1:T(8,128)(2,1)}, bf16[8,1,16,64,256]{4,2,0,3,1:T(8,128)(2,1)S(1)}, u32[]{:S(2)}) copy-start(bf16[8,1,16,64,256]{4,2,0,3,1:T(8,128)(2,1)S(1)} %copy.51) | copy-start | bytes 12582916
  159.5 4.8 %copy-start.3 = (bf16[3,3,256,256]{3,2,1,0:T(8,128)(2,1)S(1)}, bf16[3,3,256,256]{3,2,1,0:T(8,128)(2,1)}, u32[]{:S(2)}) copy-start(bf16[3,3,256,256]{3,2,1,0:T(8,128)(2,1)} %param.6) | copy-start | bytes 3538948
  191.3 4.5 %copy-start.2 = (bf16[1,128,64,256]{3,2,1,0:T(8,128)(2,1)S(1)}, bf16[1,128,64,256]{3,2,1,0:T(8,128)(2,1)}, u32[]{:S(2)}) copy-start(bf16[1,128,64,256]{3,2,1,0:T(8,128)(2,1)} %param.7) | copy-start | bytes 12582916
Sparse Core Ops, SparseCore 0:
  243.5 97.8 reduce-scatter.1
where the time goes:
time: 355 us; the launch traced here: 348 us
  matrix products  135 us (38%)
  blocking collectives  98.4 us (28%)
  waiting for transfers between devices  58.8 us (17%)
  local copies, waits for them, and re-layouts  37 us (10%)
  between operations  14.4 us (4%)
  starting transfers between devices  5.03 us (1%)
    all_to_all x1, blocking collectives, local(): lax.all_to_all(local_hidden.reshape(tiles, owned, half_rows, width // 2,...  98.4 us
    dot_general x9, matrix products, local(): jnp.dot(window, second_weight[tap_row, tap_col], preferred_element_type=j...  63.9 us
    reduce_scatter x1, waiting for transfers between devices, local(): lax.psum_scatter(jnp.stack(terms, axis=1).reshape(lax.axis_size(('group',...  58.8 us
    dot_general x9, matrix products, local(): lax.dot_general(selected, window, (((0,), (0,)), ((), ())), preferred_ele...  45.5 us
    dot_general x3, matrix products, first_conv(): jnp.dot(sources[tap_row], wide_kernel, preferred_element_type=jnp.float32)  14.8 us
    reshape x1, local copies, waits for them, and re-layouts, first_conv(): paired = source.reshape(images, rows // 2, 2, width // 2, 2 * inputs)  12.9 us
    dot_general x1, matrix products, first_conv(): jnp.dot(shift_cols_right(halves), narrow_kernel, preferred_element_type=j...  10.3 us
  transfers between devices with their start and end apart: 2, of which 1 were waited for; matrix products, arithmetic and copies ran while one was open for 20% of the time, Pallas kernels for 0%

commit v1 on v0

--- a/solution.py
+++ b/solution.py
@@ -49,13 +49,10 @@
     upper_row = shifted_2(maps[:, height - 1 : height], "tile", 1)
     local_hidden = first_conv(maps, upper_row, first_weight)
     half_rows = height // 2
-    arrived = lax.all_to_all(
-        local_hidden.reshape(tiles, owned, half_rows, width // 2, outputs),
-        "tile",
-        split_axis=0,
-        concat_axis=2,
-        tiled=True,
-    )
+    block = local_hidden.reshape(tiles, owned, half_rows, width // 2, outputs)
+    shards = jnp.split(block, lax.axis_size("tile"), axis=0)
+    received = lax.all_to_all(jnp.stack(shards), "tile", 0, 0)
+    arrived = jnp.concatenate(received, axis=2)
     hidden = arrived.reshape(owned, half_rows * tiles, width // 2, outputs)
     out_rows = hidden.shape[1]
     out_cols = hidden.shape[2]

time: 355 us -> 375 us (1.056)
  blocking collectives: 98.4 us -> 109 us
  local copies, waits for them, and re-layouts: 37 us -> 45.7 us
    all_to_all x1, blocking collectives: 98.4 us -> 109 us  [local(): received = lax.all_to_all(jnp.stack(shards), 'tile', 0, 0)]
    unnamed x15 -> x24, local copies, waits for them, and re-layouts: 6.66 us -> 14.2 us
where the time goes in v1:
time: 375 us; the launch traced here: 368 us
  matrix products  137 us (37%)
  blocking collectives  109 us (29%)
  waiting for transfers between devices  56.1 us (15%)
  local copies, waits for them, and re-layouts  45.7 us (12%)
  between operations  14.7 us (4%)
  starting transfers between devices  5.03 us (1%)
    all_to_all x1, blocking collectives, local(): received = lax.all_to_all(jnp.stack(shards), 'tile', 0, 0)  109 us
    dot_general x9, matrix products, local(): jnp.dot(window, second_weight[tap_row, tap_col], preferred_element_type=j...  66.8 us
    reduce_scatter x1, waiting for transfers between devices, local(): lax.psum_scatter(jnp.stack(terms, axis=1).reshape(lax.axis_size(('group',...  56.1 us
    dot_general x9, matrix products, local(): lax.dot_general(selected, window, (((0,), (0,)), ((), ())), preferred_ele...  45.4 us
    dot_general x3, matrix products, first_conv(): jnp.dot(sources[tap_row], wide_kernel, preferred_element_type=jnp.float32)  14.9 us
    unnamed x24, local copies, waits for them, and re-layouts  14.2 us
    reshape x1, local copies, waits for them, and re-layouts, first_conv(): paired = source.reshape(images, rows // 2, 2, width // 2, 2 * inputs)  12.9 us
    dot_general x1, matrix products, first_conv(): jnp.dot(shift_cols_right(halves), narrow_kernel, preferred_element_type=j...  10.3 us
  transfers between devices with their start and end apart: 2, of which 1 were waited for; matrix products, arithmetic and copies ran while one was open for 20% of the time, Pallas kernels for 0%

profile of v1, /device:TPU:0, one launch (start us, length us, event | category | flops | bytes accessed | tf_op | source)
XLA Modules:
  0.0 368.3 jit_solution(13994934485233358162)
XLA Ops:
  7.2 0.0 reduce-scatter.2.cloned.1.call-start
  7.2 1.0 slice.111
  8.2 0.0 copy-start.5
  8.2 5.0 %collective-permute-start = (bf16[8,1,128,128]{3,2,1,0:T(8,128)(2,1)S(1)}, bf16[8,1,128,128]{3,2,1,0:T(8,128)(2,1)S(1)}, u32[]{:S(2)}, u32[]{:S(2)}) collective-permute-start(bf16[8,1,128,128]{3,2,1,0:T(8,128)(2,1)S(1)} %slice.111), channel_id=1, source_target_pairs={{0,1},{1,2},{2,3},{3,4},{4,5},{5,6},{6,7},{8,9},{9,10},{10,11},{11... | collective-permute-start | bytes 786440 | tf_op jit(solution)/shard_map/ppermute | solution.py:10
  13.2 12.9 %reshape.113 = bf16[8,16,2,64,256]{4,3,2,1,0:T(8,128)(2,1)} reshape(bf16[8,32,128,128]{3,2,1,0:T(8,128)(2,1)} %param.4) | data formatting | bytes 16777216 | tf_op jit(solution)/shard_map/reshape | solution.py:26
  26.1 0.0 copy-done.5
  26.2 0.0 slice-start
  26.2 0.0 slice-start.1
  26.2 6.8 %fusion.196 = f32[8,16,64,256]{3,2,1,0:T(8,128)} fusion(bf16[256,256,1,1]{1,0,3,2:T(8,128)(2,1)S(1)} %bitcast.286, bf16[8,16,2,64,256]{4,3,2,1,0:T(8,128)(2,1)} %reshape.113), kind=kOutput, calls=%fused_computation.172 | convolution fusion | flops 1073741824 | bytes 12713984 | tf_op jit(solution)/shard_map/dot_general | solution.py:35
  33.0 0.0 slice-done
  33.0 0.0 slice-done.1
  33.1 4.5 %fusion.197 = f32[8,16,64,256]{3,2,1,0:T(8,128)} fusion(bf16[256,256,1,1]{1,0,3,2:T(8,128)(2,1)S(1)} %bitcast.285, bf16[8,16,2,64,256]{4,3,2,1,0:T(8,128)(2,1)S(1)} %bitcast.269), kind=kOutput, calls=%fused_computation.173 | convolution fusion | flops 1073741824 | bytes 12713984 | tf_op jit(solution)/shard_map/dot_general | solution.py:35
  37.5 1.2 slice_bitcast_fusion
  38.7 2.4 slice.143
  41.1 1.8 slice.146
  42.9 1.8 slice.145
  44.7 0.0 collective-permute-done
  44.7 0.1 reshape.112
  44.8 0.0 copy-start.2
  44.8 0.0 slice-start.2
  44.8 3.5 fusion.18
  48.4 0.0 copy-done.2
  48.4 0.0 slice-done.2
  48.4 10.3 %maximum_convert_fusion = bf16[8,16,64,256]{3,2,1,0:T(8,128)(2,1)} fusion(f32[8,16,64,256]{3,2,1,0:T(8,128)} %fusion.196, f32[8,16,64,256]{3,2,1,0:T(8,128)S(1)} %fusion.18, f32[8,16,64,256]{3,2,1,0:T(8,128)} %fusion.197, bf16[384,256,1,1]{1,0,3,2:T(8,128)(2,1)S(1)} %bitcast.283, bf16[8,16,64,128]{3,2,1,0:T(8,128)(2,1)} %slice.146, ...), kind=kOutput, calls=%fused_computation.6 | convolution fusion | flops 1661992960 | bytes 37945344 | tf_op jit(solution)/shard_map/dot_general | solution.py:38
  58.7 1.1 fusion.157
  59.8 1.1 fusion.156
  60.9 1.1 fusion.155
  61.9 1.1 fusion.154
  63.0 1.1 fusion.153
  64.1 1.1 fusion.152
  65.2 1.1 fusion.151
  66.3 1.1 fusion.150
  67.4 109.4 %all_to_all.5 = bf16[8,1,1,16,64,256]{5,4,3,2,1,0:T(8,128)(2,1)S(1)} all-to-all(bf16[8,1,1,16,64,256]{5,4,3,2,1,0:T(8,128)(2,1)S(1)} %fusion.150), channel_id=1, replica_groups=mesh['group'=4,'tile'=8] {'tile'}, dimensions={0} | all-to-all | bytes 8388608 | tf_op jit(solution)/shard_map/all_to_all | solution.py:54
  176.8 0.0 copy-start
  176.8 2.4 copy.27
  179.2 0.0 copy-start.1
  179.3 0.0 copy-start.4
  179.3 4.8 %pad_slice_fusion.1 = (bf16[1,130,63,256]{3,1,2,0:T(8,128)(2,1)S(1)}, bf16[1,130,63,256]{3,1,2,0:T(8,128)(2,1)S(1)}) fusion(bf16[1,128,64,256]{3,1,2,0:T(8,128)(2,1)S(1)} %copy.27), kind=kLoop, calls=%fused_computation.79 | loop fusion | bytes 12580864 | tf_op jit(solution)/shard_map/slice | solution.py:15
  184.1 0.0 copy-done.4
  184.1 4.5 %fusion.24 = f32[128,64,256]{2,0,1:T(8,128)} fusion(bf16[1,130,63,256]{3,1,2,0:T(8,128)(2,1)S(1)} %get-tuple-element.9, bf16[3,3,256,256]{3,2,1,0:T(8,128)(2,1)S(1)} %copy-done.4), kind=kOutput, calls=%fused_computation.25 | convolution fusion | flops 1073741824 | bytes 12906496 | tf_op jit(solution)/shard_map/dot_general | solution.py:65
  188.6 4.5 %fusion.36 = f32[128,64,256]{2,0,1:T(8,128)} fusion(bf16[1,130,63,256]{3,1,2,0:T(8,128)(2,1)S(1)} %get-tuple-element.9, bf16[3,3,256,256]{3,2,1,0:T(8,128)(2,1)S(1)} %copy-done.4), kind=kOutput, calls=%fused_computation.37 | convolution fusion | flops 1073741824 | bytes 12906496 | tf_op jit(solution)/shard_map/dot_general | solution.py:65
  193.1 4.5 %fusion.32 = f32[128,64,256]{2,0,1:T(8,128)} fusion(bf16[1,130,63,256]{3,1,2,0:T(8,128)(2,1)S(1)} %get-tuple-element.8, bf16[3,3,256,256]{3,2,1,0:T(8,128)(2,1)S(1)} %copy-done.4), kind=kOutput, calls=%fused_computation.33 | convolution fusion | flops 1073741824 | bytes 12906496 | tf_op jit(solution)/shard_map/dot_general | solution.py:65
  197.6 4.5 %fusion.40 = f32[128,64,256]{2,0,1:T(8,128)} fusion(bf16[1,130,63,256]{3,1,2,0:T(8,128)(2,1)S(1)} %get-tuple-element.8, bf16[3,3,256,256]{3,2,1,0:T(8,128)(2,1)S(1)} %copy-done.4), kind=kOutput, calls=%fused_computation.41 | convolution fusion | flops 1073741824 | bytes 12906496 | tf_op jit(solution)/shard_map/dot_general | solution.py:65
  202.1 4.5 %fusion.44 = f32[128,64,256]{2,0,1:T(8,128)} fusion(bf16[1,130,63,256]{3,1,2,0:T(8,128)(2,1)S(1)} %get-tuple-element.9, bf16[3,3,256,256]{3,2,1,0:T(8,128)(2,1)S(1)} %copy-done.4), kind=kOutput, calls=%fused_computation.45 | convolution fusion | flops 1073741824 | bytes 12906496 | tf_op jit(solution)/shard_map/dot_general | solution.py:65
  206.6 4.5 %fusion.52 = f32[128,64,256]{2,0,1:T(8,128)} fusion(bf16[1,130,63,256]{3,1,2,0:T(8,128)(2,1)S(1)} %get-tuple-element.8, bf16[3,3,256,256]{3,2,1,0:T(8,128)(2,1)S(1)} %copy-done.4), kind=kOutput, calls=%fused_computation.53 | convolution fusion | flops 1073741824 | bytes 12906496 | tf_op jit(solution)/shard_map/dot_general | solution.py:65
  211.1 4.5 %fusion.28 = f32[128,64,256]{2,0,1:T(8,128)} fusion(bf16[1,128,64,256]{3,1,2,0:T(8,128)(2,1)S(1)} %copy.27, bf16[3,3,256,256]{3,2,1,0:T(8,128)(2,1)S(1)} %copy-done.4), kind=kOutput, calls=%fused_computation.29 | convolution fusion | flops 1073741824 | bytes 12713984 | tf_op jit(solution)/shard_map/dot_general | solution.py:65
  215.6 0.0 copy-done.3
  215.6 5.4 %fusion.96 = f32[256,9,256]{0,2,1:T(8,128)S(1)} fusion(bf16[1,130,63,256]{3,1,2,0:T(8,128)(2,1)S(1)} %get-tuple-element.8, bf16[128,64,256]{2,1,0:T(8,128)(2,1)S(1)} %bitcast.273), kind=kOutput, calls=%fused_computation.93 | convolution fusion | flops 1073741824 | bytes 8649728 | tf_op jit(solution)/shard_map/dot_general | solution.py:76
  221.0 5.6 %fusion.102 = f32[256,9,256]{0,2,1:T(8,128)S(1)} fusion(f32[256,9,256]{0,2,1:T(8,128)S(1)} %fusion.96, bf16[1,128,64,256]{3,1,2,0:T(8,128)(2,1)S(1)} %copy.27, bf16[128,64,256]{2,1,0:T(8,128)(2,1)S(1)} %bitcast.274), kind=kOutput, calls=%fused_computation.95 | convolution fusion | flops 1073741824 | bytes 8650752 | tf_op jit(solution)/shard_map/dot_general | solution.py:76
  226.6 5.2 %fusion.108 = f32[256,9,256]{0,2,1:T(8,128)S(1)} fusion(f32[256,9,256]{0,2,1:T(8,128)S(1)} %fusion.102, bf16[1,130,63,256]{3,1,2,0:T(8,128)(2,1)S(1)} %get-tuple-element.9, bf16[128,64,256]{2,1,0:T(8,128)(2,1)S(1)} %bitcast.275), kind=kOutput, calls=%fused_computation.97 | convolution fusion | flops 1073741824 | bytes 8843264 | tf_op jit(solution)/shard_map/dot_general | solution.py:76
  231.8 5.4 %fusion.114 = f32[256,9,256]{0,2,1:T(8,128)S(1)} fusion(f32[256,9,256]{0,2,1:T(8,128)S(1)} %fusion.108, bf16[1,130,63,256]{3,1,2,0:T(8,128)(2,1)S(1)} %get-tuple-element.8, bf16[128,64,256]{2,1,0:T(8,128)(2,1)S(1)} %bitcast.276), kind=kOutput, calls=%fused_computation.99 | convolution fusion | flops 1073741824 | bytes 8843264 | tf_op jit(solution)/shard_map/dot_general | solution.py:76
  237.2 0.0 copy-done
  237.3 1.3 fusion.141
  238.6 5.5 %fusion.120 = f32[256,9,256]{0,2,1:T(8,128)S(1)} fusion(f32[256,9,256]{0,2,1:T(8,128)S(1)} %fusion.141, bf16[1,130,63,256]{3,1,2,0:T(8,128)(2,1)S(1)} %get-tuple-element.9, bf16[128,64,256]{2,1,0:T(8,128)(2,1)S(1)} %bitcast.278), kind=kOutput, calls=%fused_computation.101 | convolution fusion | flops 1073741824 | bytes 8843264 | tf_op jit(solution)/shard_map/dot_general | solution.py:76
  244.2 5.5 %fusion.126 = f32[256,9,256]{0,2,1:T(8,128)S(1)} fusion(f32[256,9,256]{0,2,1:T(8,128)S(1)} %fusion.120, bf16[1,130,63,256]{3,1,2,0:T(8,128)(2,1)S(1)} %get-tuple-element.8, bf16[128,64,256]{2,1,0:T(8,128)(2,1)S(1)} %bitcast.279), kind=kOutput, calls=%fused_computation.103 | convolution fusion | flops 1073741824 | bytes 8843264 | tf_op jit(solution)/shard_map/dot_general | solution.py:76
  249.6 0.0 copy-done.1
  249.6 5.6 %fusion.132 = f32[256,9,256]{0,2,1:T(8,128)S(1)} fusion(f32[256,9,256]{0,2,1:T(8,128)S(1)} %fusion.126, bf16[1,128,64,256]{3,1,2,0:T(8,128)(2,1)S(1)} %copy.27, bf16[128,64,256]{2,1,0:T(8,128)(2,1)S(1)} %bitcast.280), kind=kOutput, calls=%fused_computation.105 | convolution fusion | flops 1073741824 | bytes 8650752 | tf_op jit(solution)/shard_map/dot_general | solution.py:76
  255.3 5.8 %fusion.138 = f32[256,9,256]{0,2,1:T(8,128)S(1)} fusion(f32[256,9,256]{0,2,1:T(8,128)S(1)} %fusion.132, bf16[1,130,63,256]{3,1,2,0:T(8,128)(2,1)S(1)} %get-tuple-element.9, bf16[128,64,256]{2,1,0:T(8,128)(2,1)S(1)} %bitcast.281), kind=kOutput, calls=%fused_computation.107 | convolution fusion | flops 1073741824 | bytes 8843264 | tf_op jit(solution)/shard_map/dot_general | solution.py:76
  261.0 2.0 copy.45
  263.0 0.0 reduce-scatter.2.cloned.1.call-update
  263.0 6.7 %fusion.48 = f32[128,64,256]{2,0,1:T(8,128)} fusion(bf16[1,128,64,256]{3,1,2,0:T(8,128)(2,1)} %copy-done.1, bf16[3,3,256,256]{3,2,1,0:T(8,128)(2,1)S(1)} %copy-done.4), kind=kOutput, calls=%fused_computation.49 | convolution fusion | flops 1073741824 | bytes 12713984 | tf_op jit(solution)/shard_map/dot_general | solution.py:65
  269.7 28.6 %fusion.17 = bf16[1,128,64,256]{3,1,2,0:T(8,128)(2,1)} fusion(f32[128,64,256]{2,0,1:T(8,128)} %fusion.24, f32[128,64,256]{2,0,1:T(8,128)} %fusion.28, f32[128,64,256]{2,0,1:T(8,128)} %fusion.32, f32[128,64,256]{2,0,1:T(8,128)} %fusion.36, f32[128,64,256]{2,0,1:T(8,128)} %fusion.40, f32[128,64,256]{2,0,1:T(8,128)} %fusion.44, f32[128,64,256]{2,0,1:T(8,128)} %fusion.52, ...), kind=kOutput, calls=%fused_computation.16 | convolution fusion | flops 1092616192 | bytes 75628544 | tf_op jit(solution)/shard_map/dot_general | solution.py:65
  298.3 6.6 %copy.46 = bf16[1,128,64,256]{3,2,1,0:T(8,128)(2,1)} copy(bf16[1,128,64,256]{3,1,2,0:T(8,128)(2,1)} %fusion.17) | data formatting | bytes 8388608
  304.9 56.1 %reduce-scatter.2.cloned.1.call-done = f32[8,2304]{1,0:T(8,128)} async-done(((f32[256,2304]{1,0:T(8,128)}), f32[8,2304]{1,0:T(8,128)}) %reduce-scatter.2.cloned.1.call-update) | async-done | bytes 73744 | tf_op jit(solution)/shard_map/reduce_scatter | solution.py:80
  (3 shorter events, 0.0 us)
Async XLA Ops:
  7.2 353.9 %reduce-scatter.2.cloned.1.call-start = ((), (), s32[]{:S(2)}) async-start(), calls=%async_computation.2 | async-start | bytes 2433024 | tf_op jit(solution)/shard_map/reduce_scatter | solution.py:80
  8.2 18.0 %copy-start.5 = (bf16[3,3,128,256]{3,2,1,0:T(8,128)(2,1)S(1)}, bf16[3,3,128,256]{3,2,1,0:T(8,128)(2,1)}, u32[]{:S(2)}) copy-start(bf16[3,3,128,256]{3,2,1,0:T(8,128)(2,1)} %param.5) | copy-start | bytes 1769476
  8.2 36.5 %collective-permute-start = (bf16[8,1,128,128]{3,2,1,0:T(8,128)(2,1)S(1)}, bf16[8,1,128,128]{3,2,1,0:T(8,128)(2,1)S(1)}, u32[]{:S(2)}, u32[]{:S(2)}) collective-permute-start(bf16[8,1,128,128]{3,2,1,0:T(8,128)(2,1)S(1)} %slice.111), channel_id=1, source_target_pairs={{0,1},{1,2},{2,3},{3,4},{4,5},{5,6},{6,7},{8,9},{9,10},{10,11},{11... | collective-permute-start | bytes 786440 | tf_op jit(solution)/shard_map/ppermute | solution.py:10
  26.2 6.9 %slice-start = ((s8[8388608]{0:T(1024)(128)(4,1)}), s8[4194304]{0:T(1024)(128)(4,1)S(1)}, s32[]{:S(2)}) async-start(s8[8388608]{0:T(1024)(128)(4,1)} %bitcast.268), calls=%async_computation.3 | async-start | bytes 8388608
  26.2 6.9 %slice-start.1 = ((s8[8388608]{0:T(1024)(128)(4,1)}), s8[4194304]{0:T(1024)(128)(4,1)S(1)}, s32[]{:S(2)}) async-start(s8[8388608]{0:T(1024)(128)(4,1)} %bitcast.268), calls=%async_computation.4 | async-start | bytes 8388608
  44.8 3.5 copy-start.2
  44.8 3.5 slice-start.2
  176.8 60.4 %copy-start = (bf16[8,1,1,16,64,256]{5,4,3,2,1,0:T(8,128)(2,1)}, bf16[8,1,1,16,64,256]{5,4,3,2,1,0:T(8,128)(2,1)S(1)}, u32[]{:S(2)}) copy-start(bf16[8,1,1,16,64,256]{5,4,3,2,1,0:T(8,128)(2,1)S(1)} %all_to_all.5) | copy-start | bytes 12582916
  179.2 70.4 %copy-start.1 = (bf16[1,128,64,256]{3,1,2,0:T(8,128)(2,1)}, bf16[1,128,64,256]{3,1,2,0:T(8,128)(2,1)S(1)}, u32[]{:S(2)}) copy-start(bf16[1,128,64,256]{3,1,2,0:T(8,128)(2,1)S(1)} %copy.27) | copy-start | bytes 12582916
  179.3 4.8 %copy-start.4 = (bf16[3,3,256,256]{3,2,1,0:T(8,128)(2,1)S(1)}, bf16[3,3,256,256]{3,2,1,0:T(8,128)(2,1)}, u32[]{:S(2)}) copy-start(bf16[3,3,256,256]{3,2,1,0:T(8,128)(2,1)} %param.6) | copy-start | bytes 3538948
  211.1 4.5 %copy-start.3 = (bf16[1,128,64,256]{3,2,1,0:T(8,128)(2,1)S(1)}, bf16[1,128,64,256]{3,2,1,0:T(8,128)(2,1)}, u32[]{:S(2)}) copy-start(bf16[1,128,64,256]{3,2,1,0:T(8,128)(2,1)} %param.7) | copy-start | bytes 12582916
Sparse Core Ops, SparseCore 0:
  263.1 97.8 reduce-scatter.1
